TPU v7x, 32 devices: a whole 2x2x4 slice. The times are simulated.
32 devices in a mesh: groups: 2 (over y), ctx: 4 (over z), head: 4 (over x, core).
Axes of the slice: x: 2, y: 2, z: 4, core: 2. Of those that a mesh axis runs over, the one named last changes fastest.
Arguments:
- hidden_in: bfloat16 [2048, 4096], P(('groups', 'ctx'), 'head'), parts along dimension 0, may hold values from -6 to 6
- norm_gain: bfloat16 [4096], P('head'), may hold values from 0.099609375 to 1.8984375
- w_query: bfloat16 [4096, 2048], P('ctx', 'head'), may hold values from -8 to 8
- w_key: bfloat16 [4096, 512], P('ctx', 'head'), may hold values from -8 to 8
- w_value: bfloat16 [4096, 512], P('ctx', 'head'), may hold values from -0.09375 to 0.09375
- w_out: bfloat16 [2048, 4096], P('head', 'ctx'), may hold values from -3 to 3
- session_ids: int32 [2048], P('groups'), parts along dimension 0, may hold values from 0 to 3, never falling along the last dimension, each value on 1 to 512 neighbouring positions
- block_anchor: int32 [16], P('groups'), parts along dimension 0, may hold values from 0 to 7, each once
Outputs:
- block_update: bfloat16 [2048, 4096], P(('groups', 'ctx'), 'head'), parts along dimension 0
There are 2 independent parts, one for each index of `groups`. A program takes and returns all parts, laid end to end along the dimension named above; an argument that names none is the same for every part. Nothing has to cross between parts.
Inputs may be any that keep to these rules, and one draw needn't show every extreme that they name: `session_ids`: session numbers never fall along the contiguous order; 4 sessions, each of 1 to 512 tokens, one of exactly 512. `block_anchor`: each of the 8 blocks appears once.
All inputs are finite; a program needn't handle non-finite values.
Results may differ from a plain program's by a relative error of at most 0.0095.
The roundings to bfloat16 on the way count: a program that leaves them out, or rounds other values in their place, can miss the bound.
Values may be sent and summed in bfloat16 or wider, within the bound.
No kernel may reach another device: no remote copies, remote signals or barrier semaphores. Data moves between devices by JAX's collectives and lax.ppermute only.
A program may use at most 64 MiB of HBM per device.

v0:
```python
import math
import jax
import jax.numpy as jnp
from jax import lax
from jax.sharding import PartitionSpec as P

HD = 128
GROUP = 4
BLOCK = 128
norm_epsilon = 1e-05
rotary_base = 500000.0
masked_score = -1e30


def passed_along(block, axis, distance):
    devices = range(lax.axis_size(axis))
    route = [((i - distance) % len(devices), i) for i in devices]
    return lax.ppermute(block, axis, route)


def session_starts(session_ids):
    length = session_ids.shape[0]
    indices = jnp.arange(length, dtype=jnp.int32)
    fresh = jnp.concatenate([jnp.ones((1,), dtype=jnp.bool_), session_ids[1:] != session_ids[:-1]])
    return lax.cummax(jnp.where(fresh, indices, 0), axis=0)


def rotary(vectors, position):
    half_dim = vectors.shape[-1] // 2
    ladder = jnp.arange(half_dim, dtype=jnp.float32) * (2.0 / vectors.shape[-1])
    frequency = jnp.exp(-ladder * math.log(rotary_base))
    angles = position.astype(jnp.float32).reshape((-1,) + (1,) * (vectors.ndim - 1)) * frequency
    cosine = jnp.cos(angles)
    sines = jnp.sin(angles)
    first_half = vectors[..., :half_dim]
    second_half = vectors[..., half_dim:]
    return jnp.concatenate(
        [first_half * cosine - second_half * sines, second_half * cosine + first_half * sines],
        axis=-1,
    )


def attend_core(
    carry_state, query_heads, query_pos, query_seg, key_heads, value_heads, key_pos, key_seg
):
    row_max, row_sum, mixed_sum = carry_state
    scores = jnp.einsum(
        "qagd,kad->qagk", query_heads, key_heads, preferred_element_type=jnp.float32
    ) * (1.0 / math.sqrt(query_heads.shape[-1]))
    allowed = ((query_seg[:, None] == key_seg[None, :]) & (key_pos[None, :] <= query_pos[:, None]))[
        :, None, None, :
    ]
    new_max = jnp.maximum(row_max, jnp.max(jnp.where(allowed, scores, masked_score), axis=-1))
    weights = jnp.where(allowed, jnp.exp(scores - new_max[..., None]), 0.0)
    rescale = jnp.exp(row_max - new_max)
    row_sum = row_sum * rescale + jnp.sum(weights, axis=-1)
    mixed_sum = mixed_sum * rescale[..., None] + jnp.einsum(
        "qagk,kad->qagd",
        weights.astype(jnp.bfloat16),
        value_heads,
        preferred_element_type=jnp.float32,
    )
    return (new_max, row_sum, mixed_sum)


def per_device_ring(
    hidden_in, norm_gain, w_query, w_key, w_value, w_out, session_ids, block_anchor
):
    whole, gain_full = (
        lax.all_gather(hidden_in, "head", axis=1, tiled=True),
        lax.all_gather(norm_gain, "head", axis=0, tiled=True),
    )
    tok_rows = whole.shape[0]
    cycle_size = lax.axis_size("ctx")
    cycle_index = lax.axis_index("ctx")
    per_shard = tok_rows // BLOCK
    starts = session_starts(session_ids)
    seg_table = session_ids.reshape(-1, BLOCK)
    start_table = starts.reshape(-1, BLOCK)
    offsets = jnp.arange(BLOCK, dtype=jnp.int32)

    def token_info(owner):
        blocks_here = lax.dynamic_slice_in_dim(block_anchor, owner * per_shard, per_shard)
        contiguous = (blocks_here[:, None] * BLOCK + offsets[None, :]).reshape(-1)
        session = jnp.take(seg_table, blocks_here, axis=0).reshape(-1)
        position = contiguous - jnp.take(start_table, blocks_here, axis=0).reshape(-1)
        return (contiguous, session, position)

    wide = whole.astype(jnp.float32)
    normed = (
        wide
        * lax.rsqrt(jnp.mean(wide * wide, axis=-1, keepdims=True) + norm_epsilon)
        * gain_full.astype(jnp.float32)
    ).astype(jnp.bfloat16)
    key_cols = w_key.shape[1]
    kv_local = key_cols // HD
    pieces = (
        lax.all_gather(w_query, "ctx", axis=0, tiled=True),
        lax.all_gather(w_key, "ctx", axis=0, tiled=True),
        lax.all_gather(w_value, "ctx", axis=0, tiled=True),
    )
    query_raw, key_raw, value_raw = tuple(
        (jnp.dot(normed, weight_rows, preferred_element_type=jnp.float32) for weight_rows in pieces)
    )
    my_pos, my_seg, my_place = token_info(cycle_index)
    query_heads = rotary(query_raw.reshape(tok_rows, kv_local, GROUP, HD), my_place).astype(
        jnp.bfloat16
    )
    key_heads = rotary(key_raw.reshape(tok_rows, kv_local, HD), my_place).astype(jnp.bfloat16)
    value_heads = value_raw.astype(jnp.bfloat16).reshape(tok_rows, kv_local, HD)

    def attend(current_state, kv_stack, source):
        key_pos, key_seg, unused_place = token_info(source)
        return attend_core(
            current_state, query_heads, my_pos, my_seg, kv_stack[0], kv_stack[1], key_pos, key_seg
        )

    carry_state = (
        jnp.full((tok_rows, kv_local, GROUP), masked_score, jnp.float32),
        jnp.zeros((tok_rows, kv_local, GROUP), jnp.float32),
        jnp.zeros((tok_rows, kv_local, GROUP, HD), jnp.float32),
    )
    own_stack = jnp.stack([key_heads, value_heads])
    carry_state = attend(carry_state, own_stack, cycle_index)

    def cycle_turn(turn_index, loop_carry):
        current_state, moving = loop_carry
        moving = passed_along(moving, "ctx", 1)
        current_state = attend(current_state, moving, (cycle_index - turn_index) % cycle_size)
        return (current_state, moving)

    carry_state, unused_stack = lax.fori_loop(1, cycle_size, cycle_turn, (carry_state, own_stack))
    final_max, row_sum, mixed_sum = carry_state
    attended = (mixed_sum / row_sum[..., None]).astype(jnp.bfloat16).reshape(tok_rows, -1)
    terms = jnp.dot(
        attended,
        lax.all_gather(w_out, "ctx", axis=1, tiled=True),
        preferred_element_type=jnp.float32,
    )
    return lax.psum_scatter(terms.astype(jnp.bfloat16), "head", scatter_dimension=1, tiled=True)


def token_table(session_ids, block_anchor, owners_rows):
    starts = session_starts(session_ids)
    owner = jnp.arange(owners_rows, dtype=jnp.int32)
    contiguous = jnp.take(block_anchor, owner // BLOCK) * BLOCK + owner % BLOCK
    session = jnp.take(session_ids, contiguous)
    position = contiguous - jnp.take(starts, contiguous)
    return (contiguous, session, position)


def transposed(block, n):
    route = [(c * n + h, h * n + c) for c in range(n) for h in range(n)]
    return lax.ppermute(block, ("ctx", "head"), route)


def per_device_ws(hidden_in, norm_gain, w_query, w_key, w_value, w_out, session_ids, block_anchor):
    n = lax.axis_size("ctx")
    cycle_index = lax.axis_index("ctx")
    tok_rows, local_feats = hidden_in.shape
    wide = hidden_in.astype(jnp.float32)
    squares = lax.psum(jnp.sum(wide * wide, axis=-1, keepdims=True), "head")
    normed = (
        wide * lax.rsqrt(squares / (local_feats * n) + norm_epsilon) * norm_gain.astype(jnp.float32)
    ).astype(jnp.bfloat16)
    every = lax.all_gather(transposed(normed, n), "head", axis=0, tiled=True)
    q_cols, k_cols = (w_query.shape[1], w_key.shape[1])
    stacked = jnp.concatenate([w_query, w_key, w_value], axis=1)
    partial = jnp.dot(every, stacked, preferred_element_type=jnp.float32)
    mine = lax.psum_scatter(partial, "ctx", scatter_dimension=0, tiled=True)
    kv_local = k_cols // HD
    query_raw = mine[:, :q_cols].reshape(tok_rows, kv_local, GROUP, HD)
    key_raw = mine[:, q_cols : q_cols + k_cols].reshape(tok_rows, kv_local, HD)
    value_raw = mine[:, q_cols + k_cols :].reshape(tok_rows, kv_local, HD)
    contiguous, session, position = token_table(session_ids, block_anchor, tok_rows * n)
    my_pos = lax.dynamic_slice_in_dim(contiguous, cycle_index * tok_rows, tok_rows)
    my_seg = lax.dynamic_slice_in_dim(session, cycle_index * tok_rows, tok_rows)
    my_place = lax.dynamic_slice_in_dim(position, cycle_index * tok_rows, tok_rows)
    query_heads = rotary(query_raw, my_place).astype(jnp.bfloat16)
    key_heads = rotary(key_raw, my_place).astype(jnp.bfloat16)
    value_heads = value_raw.astype(jnp.bfloat16)
    kv_all = lax.all_gather(jnp.stack([key_heads, value_heads]), "ctx", axis=1, tiled=True)
    scores = jnp.einsum(
        "qagd,kad->qagk", query_heads, kv_all[0], preferred_element_type=jnp.float32
    ) * (1.0 / math.sqrt(HD))
    allowed = ((my_seg[:, None] == session[None, :]) & (contiguous[None, :] <= my_pos[:, None]))[
        :, None, None, :
    ]
    row_max = jnp.max(jnp.where(allowed, scores, masked_score), axis=-1, keepdims=True)
    weights = jnp.where(allowed, jnp.exp(scores - row_max), 0.0)
    row_sum = jnp.sum(weights, axis=-1, keepdims=True)
    mixed = jnp.einsum(
        "qagk,kad->qagd",
        weights.astype(jnp.bfloat16),
        kv_all[1],
        preferred_element_type=jnp.float32,
    )
    attended = (mixed / row_sum).astype(jnp.bfloat16).reshape(tok_rows, -1)
    att_all = lax.all_gather(attended, "ctx", axis=0, tiled=True)
    terms = jnp.dot(att_all, w_out, preferred_element_type=jnp.float32).astype(jnp.bfloat16)
    summed = lax.psum_scatter(terms, "head", scatter_dimension=0, tiled=True)
    return transposed(summed, n)


def solution(mesh):
    in_specs = (
        P(("groups", "ctx"), "head"),
        P("head"),
        P("ctx", "head"),
        P("ctx", "head"),
        P("ctx", "head"),
        P("head", "ctx"),
        P("groups"),
        P("groups"),
    )
    out_specs = P(("groups", "ctx"), "head")
    square = mesh.shape["ctx"] == mesh.shape["head"]
    per_device = per_device_ws if square else per_device_ring
    return jax.shard_map(
        per_device, mesh=mesh, in_specs=in_specs, out_specs=out_specs, check_vma=False
    )
```

profile of v0, /device:TPU:2, one launch (start us, length us, event | category | flops | bytes accessed | tf_op | source)
XLA Modules:
  0.0 255.6 jit_solution(16360974636456427770)
XLA Ops:
  6.5 0.8 convert_element_type.42
  7.3 1.2 fusion.18
  8.5 5.8 %psum.7 = f32[256,1]{0,1:T(1,128)S(1)} all-reduce(f32[256,1]{0,1:T(1,128)S(1)} %bitcast.89), channel_id=1, replica_groups=mesh['groups'=2,'ctx'=4,'head'=4] {'head'}, use_global_device_ids=true, to_apply=%region_1.0 | all-reduce | flops 256 | bytes 2048 | tf_op jit(solution)/shard_map/psum | solution.py:162
  14.3 1.2 fusion.20
  15.5 5.6 %collective-permute-start = (bf16[256,1024]{1,0:T(8,128)(2,1)S(1)}, bf16[256,1024]{1,0:T(8,128)(2,1)S(1)}, u32[]{:S(2)}, u32[]{:S(2)}) collective-permute-start(bf16[256,1024]{1,0:T(8,128)(2,1)S(1)} %fusion.20), channel_id=1, source_target_pairs={{0,0},{1,4},{2,8},{3,12},{4,1},{5,5},{6,9},{7,13},{8,2},{9,6},{10,... | collective-permute-start | bytes 1572872 | tf_op jit(solution)/shard_map/ppermute | solution.py:154
  21.2 23.8 %collective-permute-done = bf16[256,1024]{1,0:T(8,128)(2,1)S(1)} collective-permute-done((bf16[256,1024]{1,0:T(8,128)(2,1)S(1)}, bf16[256,1024]{1,0:T(8,128)(2,1)S(1)}, u32[]{:S(2)}, u32[]{:S(2)}) %collective-permute-start) | collective-permute-done | bytes 524320 | tf_op jit(solution)/shard_map/ppermute | solution.py:154
  45.0 0.8 copy-done.2
  45.8 20.0 %all-gather.3.cloned.1.call-done = bf16[1024,1024]{1,0:T(8,128)(2,1)} async-done(((bf16[256,1024]{1,0:T(8,128)(2,1)}), bf16[1024,1024]{1,0:T(8,128)(2,1)}) %all-gather.3.cloned.1.call-update) | async-done | bytes 2097168 | tf_op jit(solution)/shard_map/all_gather | solution.py:166
  65.8 5.5 %fusion.9 = f32[1024,768]{1,0:T(8,128)} fusion(bf16[1024,1024]{1,0:T(8,128)(2,1)} %all-gather.3.cloned.1.call-done, bf16[1024,128]{1,0:T(8,128)(2,1)} %param.14, bf16[1024,128]{1,0:T(8,128)(2,1)} %param.13, bf16[1024,512]{1,0:T(8,128)(2,1)} %param.12), kind=kOutput, calls=%fused_computation.13 | convolution fusion | flops 1615331328 | bytes 6815744 | tf_op jit(solution)/shard_map/dot_general | solution.py:169
  71.9 0.7 fusion.63
  72.6 4.3 %compare_select_fusion.1 = s32[1024,1]{0,1:T(1,128)S(1)} fusion(s32[]{:T(128)} %bitcast.4, s32[]{:T(128)} %bitcast.5, s32[]{:T(128)} %bitcast.6, s32[]{:T(128)} %bitcast.7, s32[]{:T(128)} %bitcast.8, s32[]{:T(128)} %bitcast.10, s32[]{:T(128)} %bitcast.9), kind=kLoop, calls=%fused_computation.58 | loop fusion | flops 23552 | bytes 4124 | tf_op jit(solution)/shard_map/jit(_take)/gather | solution.py:146
  77.0 0.7 fusion.56
  77.6 4.5 %gather_fusion.1 = s32[1024]{0:T(1024)S(1)} fusion(s32[1024]{0:T(1024)S(1)} %copy-done.1, s32[1024]{0:T(1024)S(1)} %get-tuple-element.6), kind=kCustom, calls=%fused_computation.1.clone | custom fusion | bytes 12288 | tf_op jit(solution)/shard_map/jit(_take)/gather | solution.py:147
  82.4 4.5 %gather_fusion = s32[1024]{0:T(1024)S(1)} fusion(s32[1024]{0:T(1024)S(1)} %maximum_bitcast_fusion, s32[1024]{0:T(1024)S(1)} %get-tuple-element.6), kind=kCustom, calls=%fused_computation.clone | custom fusion | bytes 12288 | tf_op jit(solution)/shard_map/jit(_take)/gather | solution.py:148
  87.1 0.5 multiply_cosine_fusion
  87.7 0.3 compare_and_fusion
  88.0 45.0 %reduce-scatter.3.cloned.1.call-done = f32[256,768]{1,0:T(8,128)} async-done(((f32[1024,768]{1,0:T(8,128)}), f32[256,768]{1,0:T(8,128)}) %reduce-scatter.3.cloned.1.call-update) | async-done | bytes 786448 | tf_op jit(solution)/shard_map/reduce_scatter | solution.py:170
  133.0 0.9 slice_bitcast_fusion.4
  133.9 0.6 fusion.43
  134.5 0.9 fusion.41
  135.5 15.2 %all_gather.10 = bf16[2,1024,1,128]{3,1,2,0:T(8,128)(2,1)S(1)} all-gather(bf16[2,256,1,128]{3,1,2,0:T(8,128)(2,1)S(1)} %pad_maximum_fusion), channel_id=1, replica_groups=mesh['groups'=2,'ctx'=4,'head'=4] {'ctx'}, dimensions={1}, use_global_device_ids=true | all-gather | bytes 655360 | tf_op jit(solution)/shard_map/all_gather | solution.py:182
  150.8 1.1 slice.74
  152.0 0.3 fusion.62
  152.5 0.9 fusion
  153.4 0.9 fusion.3
  154.3 1.7 fusion.24
  156.2 29.4 %all-gather.5.cloned.1.call-done = bf16[1024,512]{0,1:T(8,128)(2,1)} async-done(((bf16[256,512]{0,1:T(8,128)(2,1)}), bf16[1024,512]{0,1:T(8,128)(2,1)}) %all-gather.5.cloned.1.call-update) | async-done | bytes 1048592 | tf_op jit(solution)/shard_map/all_gather | solution.py:199
  185.6 3.9 %convolution_convert_fusion = bf16[1024,1024]{1,0:T(8,128)(2,1)} fusion(bf16[1024,512]{0,1:T(8,128)(2,1)} %all-gather.5.cloned.1.call-done, bf16[512,1024]{1,0:T(8,128)(2,1)S(1)} %copy-done), kind=kOutput, calls=%fused_computation.12 | convolution fusion | flops 1074790400 | bytes 4194304 | tf_op jit(solution)/shard_map/dot_general | solution.py:200
  189.4 29.3 %reduce-scatter.5.cloned.1.call-done = bf16[256,1024]{1,0:T(8,128)(2,1)} async-done(((bf16[1024,1024]{1,0:T(8,128)(2,1)}), bf16[256,1024]{1,0:T(8,128)(2,1)}) %reduce-scatter.5.cloned.1.call-update) | async-done | bytes 524304 | tf_op jit(solution)/shard_map/reduce_scatter | solution.py:201
  218.7 5.4 %collective-permute-start.1 = (bf16[256,1024]{1,0:T(8,128)(2,1)}, bf16[256,1024]{1,0:T(8,128)(2,1)S(1)}, u32[]{:S(2)}, u32[]{:S(2)}) collective-permute-start(bf16[256,1024]{1,0:T(8,128)(2,1)} %reduce-scatter.5.cloned.1.call-done), channel_id=1, source_target_pairs={{0,0},{1,4},{2,8},{3,12},{4,1},{5,5},{6,9},{7,13},{8,2},{9,6},{10,... | collective-permute-start | bytes 1572872 | tf_op jit(solution)/shard_map/ppermute | solution.py:154
  224.1 24.2 %collective-permute-done.1 = bf16[256,1024]{1,0:T(8,128)(2,1)S(1)} collective-permute-done((bf16[256,1024]{1,0:T(8,128)(2,1)}, bf16[256,1024]{1,0:T(8,128)(2,1)S(1)}, u32[]{:S(2)}, u32[]{:S(2)}) %collective-permute-start.1) | collective-permute-done | bytes 524320 | tf_op jit(solution)/shard_map/ppermute | solution.py:154
  248.3 0.8 copy.35
  (32 shorter events, 1.6 us)
Async XLA Ops:
  6.5 179.0 %copy-start = (bf16[512,1024]{1,0:T(8,128)(2,1)S(1)}, bf16[512,1024]{1,0:T(8,128)(2,1)}, u32[]{:S(2)}) copy-start(bf16[512,1024]{1,0:T(8,128)(2,1)} %param.15) | copy-start | bytes 3145732
  6.5 59.3 %all-gather.3.cloned.1.call-start = ((), (), s32[]{:S(2)}) async-start(), calls=%async_computation.2 | async-start | bytes 2621440 | tf_op jit(solution)/shard_map/all_gather | solution.py:166
  15.5 29.4 %collective-permute-start = (bf16[256,1024]{1,0:T(8,128)(2,1)S(1)}, bf16[256,1024]{1,0:T(8,128)(2,1)S(1)}, u32[]{:S(2)}, u32[]{:S(2)}) collective-permute-start(bf16[256,1024]{1,0:T(8,128)(2,1)S(1)} %fusion.20), channel_id=1, source_target_pairs={{0,0},{1,4},{2,8},{3,12},{4,1},{5,5},{6,9},{7,13},{8,2},{9,6},{10,... | collective-permute-start | bytes 1572872 | tf_op jit(solution)/shard_map/ppermute | solution.py:154
  45.0 0.8 copy-start.2
  45.8 25.6 %copy-start.1 = (s32[1024]{0:T(1024)S(1)}, s32[1024]{0:T(1024)}, u32[]{:S(2)}) copy-start(s32[1024]{0:T(1024)} %param.16) | copy-start | bytes 12292
  45.8 26.2 %copy-start.3 = (s32[8]{0:T(128)S(1)}, s32[8]{0:T(128)}, u32[]{:S(2)}) copy-start(s32[8]{0:T(128)} %param.17) | copy-start | bytes 100
  45.8 87.2 %reduce-scatter.3.cloned.1.call-start = ((), (), s32[]{:S(2)}) async-start(), calls=%async_computation.3 | async-start | bytes 3932160 | tf_op jit(solution)/shard_map/reduce_scatter | solution.py:170
  71.3 114.2 %all-gather.5.cloned.1.call-start = ((), (), s32[]{:S(2)}) async-start(), calls=%async_computation.4 | async-start | bytes 1310720 | tf_op jit(solution)/shard_map/all_gather | solution.py:199
  156.1 62.6 %reduce-scatter.5.cloned.1.call-start = ((), (), s32[]{:S(2)}) async-start(), calls=%async_computation.5 | async-start | bytes 2621440 | tf_op jit(solution)/shard_map/reduce_scatter | solution.py:201
  218.7 29.6 %collective-permute-start.1 = (bf16[256,1024]{1,0:T(8,128)(2,1)}, bf16[256,1024]{1,0:T(8,128)(2,1)S(1)}, u32[]{:S(2)}, u32[]{:S(2)}) collective-permute-start(bf16[256,1024]{1,0:T(8,128)(2,1)} %reduce-scatter.5.cloned.1.call-done), channel_id=1, source_target_pairs={{0,0},{1,4},{2,8},{3,12},{4,1},{5,5},{6,9},{7,13},{8,2},{9,6},{10,... | collective-permute-start | bytes 1572872 | tf_op jit(solution)/shard_map/ppermute | solution.py:154
Sparse Core Ops, SparseCore 0:
  45.9 19.8 all-gather.2
  71.4 61.5 reduce-scatter.2
  156.2 29.2 all-gather.4
  189.6 29.1 reduce-scatter.4
where the time goes:
time: 256 us
  waiting for transfers between devices  172 us (67%)
  blocking collectives  21 us (8%)
  local copies, waits for them, and re-layouts  15.1 us (6%)
  between operations  13.3 us (5%)
  matrix products  12 us (5%)
  other arithmetic  11.5 us (4%)
  starting transfers between devices  11.1 us (4%)
    ppermute x2, waiting for transfers between devices, transposed(): return lax.ppermute(block, ('ctx', 'head'), route)  48 us
    reduce_scatter x1, waiting for transfers between devices, per_device_ws(): mine = lax.psum_scatter(partial, 'ctx', scatter_dimension=0, tiled=True)  45 us
    all_gather x1, waiting for transfers between devices, per_device_ws(): att_all = lax.all_gather(attended, 'ctx', axis=0, tiled=True)  29.4 us
    reduce_scatter x1, waiting for transfers between devices, per_device_ws(): summed = lax.psum_scatter(terms, 'head', scatter_dimension=0, tiled=True)  29.3 us
    all_gather x1, waiting for transfers between devices, per_device_ws(): every = lax.all_gather(transposed(normed, n), 'head', axis=0, tiled=True)  20 us
    all_gather x1, blocking collectives, per_device_ws(): lax.all_gather(jnp.stack([key_heads, value_heads]), 'ctx', axis=1, tiled=...  15.2 us
    ppermute x2, starting transfers between devices, transposed(): return lax.ppermute(block, ('ctx', 'head'), route)  11 us
    psum x1, blocking collectives, per_device_ws(): squares = lax.psum(jnp.sum(wide * wide, axis=-1, keepdims=True), 'head')  5.77 us
  transfers between devices with their start and end apart: 6, of which 6 were waited for; matrix products, arithmetic and copies ran while one was open for 6% of the time, Pallas kernels for 0%

commit v1 on v0

--- a/solution.py
+++ b/solution.py
@@ -1,8 +1,10 @@
+import functools
 import math
 import jax
 import jax.numpy as jnp
 from jax import lax
 from jax.sharding import PartitionSpec as P
+from jax.lax import axis_index, axis_size, ppermute
 
 HD = 128
 GROUP = 4
@@ -10,6 +12,41 @@
 norm_epsilon = 1e-05
 rotary_base = 500000.0
 masked_score = -1e30
+
+
+def _fill_stocks(packet, dim_i):
+    z = list(packet.shape[1:])
+    z[dim_i] *= packet.shape[0]
+    f_next = jnp.moveaxis(packet, 0, dim_i).reshape(z)
+    return f_next
+
+
+def groups_note(xx, peer_axis, ndim_at):
+    cores_n = axis_size(peer_axis)
+    y1 = range(cores_n)
+    after = map(lambda src_i: (src_i, (src_i + 1) % cores_n), y1)
+    series = list(after)
+    all_blocks = [(j0, rr) for rr, j0 in series]
+    block_out, ready = ([], [])
+    t = 0
+    while t < cores_n - 1:
+        if t % 2 == 0:
+            p_next = ppermute(block_out[-1] if block_out else xx, peer_axis, perm=series)
+            block_out.append(p_next)
+        else:
+            piece_out = ppermute(ready[-1] if ready else xx, peer_axis, all_blocks)
+            ready.append(piece_out)
+        t += 1
+    a_now = jnp.stack([*block_out[::-1], xx, *ready])
+    reply = axis_index(peer_axis)
+    next_value = len(block_out)
+    state_next = reply - next_value
+    a_now = a_now[(jnp.arange(cores_n) - state_next) % cores_n]
+    x_now = _fill_stocks(a_now, ndim_at)
+    return x_now
+
+
+post_the_page = functools.partial(groups_note, peer_axis="head", ndim_at=0)
 
 
 def passed_along(block, axis, distance):
@@ -163,7 +200,7 @@
     normed = (
         wide * lax.rsqrt(squares / (local_feats * n) + norm_epsilon) * norm_gain.astype(jnp.float32)
     ).astype(jnp.bfloat16)
-    every = lax.all_gather(transposed(normed, n), "head", axis=0, tiled=True)
+    every = post_the_page(transposed(normed, n))
     q_cols, k_cols = (w_query.shape[1], w_key.shape[1])
     stacked = jnp.concatenate([w_query, w_key, w_value], axis=1)
     partial = jnp.dot(every, stacked, preferred_element_type=jnp.float32)

time: 256 us -> 258 us (level)
  waiting for transfers between devices: 172 us -> 169 us
    all_gather x1 -> x0, waiting for transfers between devices: 20 us -> none  [per_device_ws(): every = lax.all_gather(transposed(normed, n), 'head', axis=0, tiled=True)]
    ppermute x0 -> x3, waiting for transfers between devices: none -> 15.4 us  [the longest x2 10.5 us: groups_note(): ppermute(block_out[-1] if block_out else xx, peer_axis, perm=series)]
  transfers between devices with their start and end apart: 6 -> 8, of which waited for: 6 -> 8; matrix products, arithmetic and copies ran while one was open for 6% -> 6% of each run, Pallas kernels for 0% -> 0%
where the time goes in v1:
time: 258 us
  waiting for transfers between devices  169 us (66%)
  blocking collectives  21 us (8%)
  local copies, waits for them, and re-layouts  16.7 us (6%)
  other arithmetic  13.3 us (5%)
  between operations  13.3 us (5%)
  starting transfers between devices  12.8 us (5%)
  matrix products  11.9 us (5%)
    ppermute x2, waiting for transfers between devices, transposed(): return lax.ppermute(block, ('ctx', 'head'), route)  48.1 us
    reduce_scatter x1, waiting for transfers between devices, per_device_ws(): mine = lax.psum_scatter(partial, 'ctx', scatter_dimension=0, tiled=True)  46.3 us
    all_gather x1, waiting for transfers between devices, per_device_ws(): att_all = lax.all_gather(attended, 'ctx', axis=0, tiled=True)  29.4 us
    reduce_scatter x1, waiting for transfers between devices, per_device_ws(): summed = lax.psum_scatter(terms, 'head', scatter_dimension=0, tiled=True)  29.3 us
    all_gather x1, blocking collectives, per_device_ws(): lax.all_gather(jnp.stack([key_heads, value_heads]), 'ctx', axis=1, tiled=...  15.3 us
    ppermute x2, starting transfers between devices, transposed(): return lax.ppermute(block, ('ctx', 'head'), route)  11 us
    ppermute x2, waiting for transfers between devices, groups_note(): ppermute(block_out[-1] if block_out else xx, peer_axis, perm=series)  10.5 us
    psum x1, blocking collectives, per_device_ws(): squares = lax.psum(jnp.sum(wide * wide, axis=-1, keepdims=True), 'head')  5.77 us
  transfers between devices with their start and end apart: 8, of which 8 were waited for; matrix products, arithmetic and copies ran while one was open for 6% of the time, Pallas kernels for 0%

profile of v1, /device:TPU:2, one launch (start us, length us, event | category | flops | bytes accessed | tf_op | source)
XLA Modules:
  0.0 257.5 jit_solution(3044271662013856566)
XLA Ops:
  6.5 0.8 convert_element_type.42
  7.3 1.2 fusion.18
  8.5 5.8 %psum.7 = f32[256,1]{0,1:T(1,128)S(1)} all-reduce(f32[256,1]{0,1:T(1,128)S(1)} %bitcast.101), channel_id=1, replica_groups=mesh['groups'=2,'ctx'=4,'head'=4] {'head'}, use_global_device_ids=true, to_apply=%region_1.0 | all-reduce | flops 256 | bytes 2048 | tf_op jit(solution)/shard_map/psum | solution.py:199
  14.3 1.2 fusion.20
  15.5 5.6 %collective-permute-start = (bf16[256,1024]{1,0:T(8,128)(2,1)S(1)}, bf16[256,1024]{1,0:T(8,128)(2,1)S(1)}, u32[]{:S(2)}, u32[]{:S(2)}) collective-permute-start(bf16[256,1024]{1,0:T(8,128)(2,1)S(1)} %fusion.20), channel_id=1, source_target_pairs={{0,0},{1,4},{2,8},{3,12},{4,1},{5,5},{6,9},{7,13},{8,2},{9,6},{10,... | collective-permute-start | bytes 1572872 | tf_op jit(solution)/shard_map/ppermute | solution.py:191
  21.2 23.9 %collective-permute-done = bf16[256,1024]{1,0:T(8,128)(2,1)S(1)} collective-permute-done((bf16[256,1024]{1,0:T(8,128)(2,1)S(1)}, bf16[256,1024]{1,0:T(8,128)(2,1)S(1)}, u32[]{:S(2)}, u32[]{:S(2)}) %collective-permute-start) | collective-permute-done | bytes 524320 | tf_op jit(solution)/shard_map/ppermute | solution.py:191
  45.1 1.7 collective-permute-start.3
  46.8 6.9 %collective-permute-done.1 = bf16[256,1024]{1,0:T(8,128)(2,1)S(1)} collective-permute-done((bf16[256,1024]{1,0:T(8,128)(2,1)S(1)}, bf16[256,1024]{1,0:T(8,128)(2,1)S(1)}, u32[]{:S(2)}, u32[]{:S(2)}) %collective-permute-start.1) | collective-permute-done | bytes 524320 | tf_op jit(solution)/shard_map/ppermute | solution.py:34
  53.7 4.9 %collective-permute-done.3 = bf16[256,1024]{1,0:T(8,128)(2,1)S(1)} collective-permute-done((bf16[256,1024]{1,0:T(8,128)(2,1)S(1)}, bf16[256,1024]{1,0:T(8,128)(2,1)S(1)}, u32[]{:S(2)}, u32[]{:S(2)}) %collective-permute-start.3) | collective-permute-done | bytes 524320 | tf_op jit(solution)/shard_map/ppermute | solution.py:37
  58.6 3.7 %collective-permute-done.2 = bf16[256,1024]{1,0:T(8,128)(2,1)S(1)} collective-permute-done((bf16[256,1024]{1,0:T(8,128)(2,1)S(1)}, bf16[256,1024]{1,0:T(8,128)(2,1)S(1)}, u32[]{:S(2)}, u32[]{:S(2)}) %collective-permute-start.2) | collective-permute-done | bytes 524320 | tf_op jit(solution)/shard_map/ppermute | solution.py:34
  62.3 0.8 copy-done.5
  63.1 1.8 pad_maximum_fusion
  64.9 2.0 gather_fusion
  66.9 5.4 %fusion.9 = f32[1024,768]{1,0:T(8,128)} fusion(bf16[1024,1024]{1,0:T(8,128)(2,1)} %bitcast.93, bf16[1024,128]{1,0:T(8,128)(2,1)S(1)} %copy-done.7, bf16[1024,128]{1,0:T(8,128)(2,1)} %param.13, bf16[1024,512]{1,0:T(8,128)(2,1)} %param.12), kind=kOutput, calls=%fused_computation.15 | convolution fusion | flops 1615331328 | bytes 6815744 | tf_op jit(solution)/shard_map/dot_general | solution.py:206
  73.5 0.7 fusion.65
  74.2 4.3 %compare_select_fusion.1 = s32[1024,1]{0,1:T(1,128)S(1)} fusion(s32[]{:T(128)} %bitcast.10, s32[]{:T(128)} %bitcast.11, s32[]{:T(128)} %bitcast.12, s32[]{:T(128)} %bitcast.13, s32[]{:T(128)} %bitcast.14, s32[]{:T(128)} %bitcast.16, s32[]{:T(128)} %bitcast.15), kind=kLoop, calls=%fused_computation.60 | loop fusion | flops 23552 | bytes 4124 | tf_op jit(solution)/shard_map/jit(_take)/gather | solution.py:183
  78.6 0.7 fusion.56
  79.2 4.5 %gather_fusion.2 = s32[1024]{0:T(1024)S(1)} fusion(s32[1024]{0:T(1024)S(1)} %copy-done.1, s32[1024]{0:T(1024)S(1)} %get-tuple-element.6), kind=kCustom, calls=%fused_computation.1.clone | custom fusion | bytes 12288 | tf_op jit(solution)/shard_map/jit(_take)/gather | solution.py:184
  84.0 4.5 %gather_fusion.1 = s32[1024]{0:T(1024)S(1)} fusion(s32[1024]{0:T(1024)S(1)} %maximum_bitcast_fusion, s32[1024]{0:T(1024)S(1)} %get-tuple-element.6), kind=kCustom, calls=%fused_computation.clone | custom fusion | bytes 12288 | tf_op jit(solution)/shard_map/jit(_take)/gather | solution.py:185
  89.6 46.3 %reduce-scatter.3.cloned.1.call-done = f32[256,768]{1,0:T(8,128)} async-done(((f32[1024,768]{1,0:T(8,128)}), f32[256,768]{1,0:T(8,128)}) %reduce-scatter.3.cloned.1.call-update) | async-done | bytes 786448 | tf_op jit(solution)/shard_map/reduce_scatter | solution.py:207
  135.9 1.0 slice_bitcast_fusion.4
  137.5 0.9 fusion.41
  138.5 15.3 %all_gather.6 = bf16[2,1024,1,128]{3,1,2,0:T(8,128)(2,1)S(1)} all-gather(bf16[2,256,1,128]{3,1,2,0:T(8,128)(2,1)S(1)} %pad_maximum_fusion.1), channel_id=1, replica_groups=mesh['groups'=2,'ctx'=4,'head'=4] {'ctx'}, dimensions={1}, use_global_device_ids=true | all-gather | bytes 655360 | tf_op jit(solution)/shard_map/all_gather | solution.py:219
  154.4 0.9 fusion
  155.3 0.9 fusion.3
  156.2 1.7 fusion.24
  158.1 29.4 %all-gather.2.cloned.1.call-done = bf16[1024,512]{0,1:T(8,128)(2,1)} async-done(((bf16[256,512]{0,1:T(8,128)(2,1)}), bf16[1024,512]{0,1:T(8,128)(2,1)}) %all-gather.2.cloned.1.call-update) | async-done | bytes 1048592 | tf_op jit(solution)/shard_map/all_gather | solution.py:236
  187.5 3.9 %convolution_convert_fusion = bf16[1024,1024]{1,0:T(8,128)(2,1)} fusion(bf16[1024,512]{0,1:T(8,128)(2,1)} %all-gather.2.cloned.1.call-done, bf16[512,1024]{1,0:T(8,128)(2,1)S(1)} %copy-done), kind=kOutput, calls=%fused_computation.14 | convolution fusion | flops 1074790400 | bytes 4194304 | tf_op jit(solution)/shard_map/dot_general | solution.py:237
  191.3 29.3 %reduce-scatter.5.cloned.1.call-done = bf16[256,1024]{1,0:T(8,128)(2,1)} async-done(((bf16[1024,1024]{1,0:T(8,128)(2,1)}), bf16[256,1024]{1,0:T(8,128)(2,1)}) %reduce-scatter.5.cloned.1.call-update) | async-done | bytes 524304 | tf_op jit(solution)/shard_map/reduce_scatter | solution.py:238
  220.6 5.4 %collective-permute-start.4 = (bf16[256,1024]{1,0:T(8,128)(2,1)}, bf16[256,1024]{1,0:T(8,128)(2,1)S(1)}, u32[]{:S(2)}, u32[]{:S(2)}) collective-permute-start(bf16[256,1024]{1,0:T(8,128)(2,1)} %reduce-scatter.5.cloned.1.call-done), channel_id=1, source_target_pairs={{0,0},{1,4},{2,8},{3,12},{4,1},{5,5},{6,9},{7,13},{8,2},{9,6},{10,... | collective-permute-start | bytes 1572872 | tf_op jit(solution)/shard_map/ppermute | solution.py:191
  226.1 24.2 %collective-permute-done.4 = bf16[256,1024]{1,0:T(8,128)(2,1)S(1)} collective-permute-done((bf16[256,1024]{1,0:T(8,128)(2,1)}, bf16[256,1024]{1,0:T(8,128)(2,1)S(1)}, u32[]{:S(2)}, u32[]{:S(2)}) %collective-permute-start.4) | collective-permute-done | bytes 524320 | tf_op jit(solution)/shard_map/ppermute | solution.py:191
  250.2 0.8 copy.35
  (48 shorter events, 4.0 us)
Async XLA Ops:
  6.5 180.9 %copy-start = (bf16[512,1024]{1,0:T(8,128)(2,1)S(1)}, bf16[512,1024]{1,0:T(8,128)(2,1)}, u32[]{:S(2)}) copy-start(bf16[512,1024]{1,0:T(8,128)(2,1)} %param.15) | copy-start | bytes 3145732
  6.5 129.4 %reduce-scatter.3.cloned.1.call-start = ((), (), s32[]{:S(2)}) async-start(), calls=%async_computation.2 | async-start | bytes 3932160 | tf_op jit(solution)/shard_map/reduce_scatter | solution.py:207
  15.5 29.5 %collective-permute-start = (bf16[256,1024]{1,0:T(8,128)(2,1)S(1)}, bf16[256,1024]{1,0:T(8,128)(2,1)S(1)}, u32[]{:S(2)}, u32[]{:S(2)}) collective-permute-start(bf16[256,1024]{1,0:T(8,128)(2,1)S(1)} %fusion.20), channel_id=1, source_target_pairs={{0,0},{1,4},{2,8},{3,12},{4,1},{5,5},{6,9},{7,13},{8,2},{9,6},{10,... | collective-permute-start | bytes 1572872 | tf_op jit(solution)/shard_map/ppermute | solution.py:191
  45.0 17.2 %copy-start.2 = (bf16[256,1024]{1,0:T(8,128)(2,1)}, bf16[256,1024]{1,0:T(8,128)(2,1)S(1)}, u32[]{:S(2)}) copy-start(bf16[256,1024]{1,0:T(8,128)(2,1)S(1)} %collective-permute-done) | copy-start | bytes 1572868
  45.1 8.6 %collective-permute-start.1 = (bf16[256,1024]{1,0:T(8,128)(2,1)S(1)}, bf16[256,1024]{1,0:T(8,128)(2,1)S(1)}, u32[]{:S(2)}, u32[]{:S(2)}) collective-permute-start(bf16[256,1024]{1,0:T(8,128)(2,1)S(1)} %collective-permute-done), channel_id=1, source_target_pairs={{0,1},{1,2},{2,3},{3,0},{4,5},{5,6},{6,7},{7,4},{8,9},{9,10},{10,1... | collective-permute-start | bytes 1572872 | tf_op jit(solution)/shard_map/ppermute | solution.py:34
  45.1 13.5 %collective-permute-start.3 = (bf16[256,1024]{1,0:T(8,128)(2,1)S(1)}, bf16[256,1024]{1,0:T(8,128)(2,1)S(1)}, u32[]{:S(2)}, u32[]{:S(2)}) collective-permute-start(bf16[256,1024]{1,0:T(8,128)(2,1)S(1)} %collective-permute-done), channel_id=1, source_target_pairs={{1,0},{2,1},{3,2},{0,3},{5,4},{6,5},{7,6},{4,7},{9,8},{10,9},{11,1... | collective-permute-start | bytes 1572872 | tf_op jit(solution)/shard_map/ppermute | solution.py:37
  53.7 8.6 %copy-start.3 = (bf16[256,1024]{1,0:T(8,128)(2,1)}, bf16[256,1024]{1,0:T(8,128)(2,1)S(1)}, u32[]{:S(2)}) copy-start(bf16[256,1024]{1,0:T(8,128)(2,1)S(1)} %collective-permute-done.1) | copy-start | bytes 1572868
  53.7 8.6 %collective-permute-start.2 = (bf16[256,1024]{1,0:T(8,128)(2,1)S(1)}, bf16[256,1024]{1,0:T(8,128)(2,1)S(1)}, u32[]{:S(2)}, u32[]{:S(2)}) collective-permute-start(bf16[256,1024]{1,0:T(8,128)(2,1)S(1)} %collective-permute-done.1), channel_id=1, source_target_pairs={{0,1},{1,2},{2,3},{3,0},{4,5},{5,6},{6,7},{7,4},{8,9},{9,10},{10,1... | collective-permute-start | bytes 1572872 | tf_op jit(solution)/shard_map/ppermute | solution.py:34
  58.6 3.7 %copy-start.4 = (bf16[256,1024]{1,0:T(8,128)(2,1)}, bf16[256,1024]{1,0:T(8,128)(2,1)S(1)}, u32[]{:S(2)}) copy-start(bf16[256,1024]{1,0:T(8,128)(2,1)S(1)} %collective-permute-done.3) | copy-start | bytes 1572868
  62.3 0.8 copy-start.5
  64.8 2.1 copy-start.7
  72.3 0.7 copy-start.1
  72.3 1.3 copy-start.6
  72.3 115.2 %all-gather.2.cloned.1.call-start = ((), (), s32[]{:S(2)}) async-start(), calls=%async_computation.3 | async-start | bytes 1310720 | tf_op jit(solution)/shard_map/all_gather | solution.py:236
  135.9 17.8 %slice-start = ((f32[256,768]{1,0:T(8,128)}), f32[256,512]{1,0:T(8,128)S(1)}, s32[]{:S(2)}) async-start(f32[256,768]{1,0:T(8,128)} %reduce-scatter.3.cloned.1.call-done), calls=%async_computation.5 | async-start | bytes 1048576 | tf_op jit(solution)/shard_map/slice | solution.py:209
  158.0 62.6 %reduce-scatter.5.cloned.1.call-start = ((), (), s32[]{:S(2)}) async-start(), calls=%async_computation.4 | async-start | bytes 2621440 | tf_op jit(solution)/shard_map/reduce_scatter | solution.py:238
  220.6 29.6 %collective-permute-start.4 = (bf16[256,1024]{1,0:T(8,128)(2,1)}, bf16[256,1024]{1,0:T(8,128)(2,1)S(1)}, u32[]{:S(2)}, u32[]{:S(2)}) collective-permute-start(bf16[256,1024]{1,0:T(8,128)(2,1)} %reduce-scatter.5.cloned.1.call-done), channel_id=1, source_target_pairs={{0,0},{1,4},{2,8},{3,12},{4,1},{5,5},{6,9},{7,13},{8,2},{9,6},{10,... | collective-permute-start | bytes 1572872 | tf_op jit(solution)/shard_map/ppermute | solution.py:191
Sparse Core Ops, SparseCore 0:
  72.4 63.4 reduce-scatter.2
  158.1 29.2 all-gather.1
  191.5 29.1 reduce-scatter.4
